TPU v7x, 32 devices: a whole 2x2x4 slice. The times are simulated.
32 devices in a mesh: groups: 2 (over y), seq: 16 (over z, x, core).
Axes of the slice: x: 2, y: 2, z: 4, core: 2. Of those that a mesh axis runs over, the one named last changes fastest.
Arguments:
- query_rows: bfloat16 [4096, 768], P(('groups', 'seq')), parts along dimension 0, may hold values from -10 to 10
- key_rows: bfloat16 [4096, 768], P(('groups', 'seq')), parts along dimension 0, may hold values from -10 to 10
- value_rows: bfloat16 [4096, 768], P(('groups', 'seq')), parts along dimension 0, may hold values from -6 to 6
- output_grad: bfloat16 [4096, 768], P(('groups', 'seq')), parts along dimension 0, may hold values from -6 to 6
- head_offsets: int32 [3, 12], replicated, may hold values from 0 to 15, as said below
Outputs:
- attended: bfloat16 [4096, 768], P(('groups', 'seq')), parts along dimension 0
- query_grad: bfloat16 [4096, 768], P(('groups', 'seq')), parts along dimension 0
- key_grad: bfloat16 [4096, 768], P(('groups', 'seq')), parts along dimension 0
- value_grad: bfloat16 [4096, 768], P(('groups', 'seq')), parts along dimension 0
There are 2 independent parts, one for each index of `groups`. A program takes and returns all parts, laid end to end along the dimension named above; an argument that names none is the same for every part. Nothing has to cross between parts.
Inputs may be any that keep to these rules, and one draw needn't show every extreme that they name: `head_offsets`: row 0 is all zeros; the entries of row 1 lie below 4, those of row 2 below 16.
All inputs are finite; a program needn't handle non-finite values.
Results may differ from a plain program's by a relative error of at most 0.0084.
Values may be sent and summed in bfloat16 or wider, within the bound.
No kernel may reach another device: no remote copies, remote signals or barrier semaphores. Data moves between devices by JAX's collectives and lax.ppermute only.
A program may use at most 128 MiB of HBM per device.

v0:
```python
import math

import numpy as np
import jax
import jax.numpy as jnp
from jax import lax
from jax.sharding import Mesh, NamedSharding, PartitionSpec as P

LEN_NEAR = 1024
LEN_MID = 4096
LEN_FAR = 16384
DILATION_FIRST = 1
DILATION_SECOND = 4
DILATION_THIRD = 16

NEG_FILL = -1e30


def segment_plan(seq_devices, local_rows):
    tokens_all = seq_devices * local_rows
    seg_lengths = [min(LEN_NEAR, tokens_all), min(LEN_MID, tokens_all), min(LEN_FAR, tokens_all)]
    spans = [seg_length // local_rows for seg_length in seg_lengths]
    distinct = sorted(set(spans))
    factors = []
    previous = 1
    for span in distinct:
        factors.append(span // previous)
        previous = span
    outer = seq_devices // previous
    names = ["q%d" % k for k in range(len(distinct), -1, -1)]
    sizes = [outer] + factors[::-1]
    branch_axes = []
    for span in spans:
        level = distinct.index(span)
        branch_axes.append(tuple(names[len(names) - 1 - level :]))
    return names, sizes, branch_axes


def pick_rows(rows, stride, offsets_row):
    count, heads, dim = rows.shape
    grouped = rows.reshape(count // stride, stride, heads, dim)
    chosen = (jnp.arange(stride, dtype=jnp.int32)[:, None] == offsets_row[None, :])[None, :, :, None]
    return jnp.sum(jnp.where(chosen, grouped, jnp.zeros((), rows.dtype)), axis=1)


def spread_rows(picked, stride, offsets_row):
    count, heads, dim = picked.shape
    chosen = (jnp.arange(stride, dtype=jnp.int32)[:, None] == offsets_row[None, :])[None, :, :, None]
    widened = jnp.where(chosen, picked[:, None], jnp.zeros((), picked.dtype))
    return widened.reshape(count * stride, heads, dim)


def make_per_device(branch_axes):
    strides = [DILATION_FIRST, DILATION_SECOND, DILATION_THIRD]
    groups = []
    for branch, axes in enumerate(branch_axes):
        for entry in groups:
            if entry[0] == axes:
                entry[1].append(branch)
                break
        else:
            groups.append((axes, [branch]))

    def per_device(query_rows, key_rows, value_rows, output_grad, head_offsets):
        local_rows, model_width = query_rows.shape
        head_count = head_offsets.shape[1]
        head_dim = model_width // head_count
        score_scale = 1.0 / math.sqrt(head_dim)
        shape3 = (local_rows, head_count, head_dim)
        query3 = query_rows.reshape(shape3)
        key3 = key_rows.reshape(shape3)
        value3 = value_rows.reshape(shape3)
        grad3 = output_grad.reshape(shape3)
        kv3 = jnp.stack([key3, value3])

        gathered = [None] * 3
        for axes, members in groups:
            parts = [
                jax.vmap(lambda block, b=branch: pick_rows(block, strides[b], head_offsets[b]))(kv3)
                for branch in members
            ]
            counts = [part.shape[1] for part in parts]
            joined = jnp.concatenate(parts, axis=1)
            full = lax.all_gather(joined, axes, axis=1, tiled=False)
            cursor = 0
            for branch, count in zip(members, counts):
                block = full[:, :, cursor : cursor + count]
                gathered[branch] = block.reshape(2, -1, head_count, head_dim)
                cursor += count
        key_counts = [block.shape[1] for block in gathered]
        kv_all = jnp.concatenate(gathered, axis=1)
        key_all = kv_all[0]
        value_all = kv_all[1]

        local_index = jnp.arange(local_rows, dtype=jnp.int32)
        member = [
            (local_index[None, :] % strides[branch]) == head_offsets[branch][:, None]
            for branch in range(3)
        ]
        key_branch = np.concatenate(
            [np.full((count,), branch, np.int32) for branch, count in enumerate(key_counts)]
        )
        valid = None
        for branch in range(3):
            term = member[branch][:, :, None] & jnp.asarray(key_branch == branch)[None, None, :]
            valid = term if valid is None else valid | term

        scores = (
            jnp.einsum("qhe,khe->hqk", query3, key_all, preferred_element_type=jnp.float32)
            * score_scale
        )
        scores = jnp.where(valid, scores, NEG_FILL)
        peak = jnp.max(scores, axis=2, keepdims=True)
        expo = jnp.where(valid, jnp.exp(scores - peak), 0.0)
        total = jnp.sum(expo, axis=2, keepdims=True)
        prob = expo / total
        weight = prob.astype(jnp.bfloat16)
        mixed = jnp.einsum("hqk,khe->qhe", weight, value_all, preferred_element_type=jnp.float32)
        balance = jnp.sum(grad3.astype(jnp.float32) * mixed, axis=2)
        flow = jnp.einsum("qhe,khe->hqk", grad3, value_all, preferred_element_type=jnp.float32)
        score_grad = (prob * (flow - jnp.transpose(balance)[:, :, None])).astype(jnp.bfloat16)
        query_grad = (
            jnp.einsum("hqk,khe->qhe", score_grad, key_all, preferred_element_type=jnp.float32)
            * score_scale
        )
        key_terms = (
            jnp.einsum("hqk,qhe->khe", score_grad, query3, preferred_element_type=jnp.float32)
            * score_scale
        )
        value_terms = jnp.einsum("hqk,qhe->khe", weight, grad3, preferred_element_type=jnp.float32)
        terms = jnp.stack([key_terms, value_terms])

        starts = np.cumsum([0] + key_counts)
        total_grad = None
        for axes, members in groups:
            blocks = [terms[:, starts[branch] : starts[branch + 1]] for branch in members]
            dev_count = 1
            for name in axes:
                dev_count *= lax.axis_size(name)
            shaped = [
                block.reshape(2, dev_count, -1, head_count, head_dim) for block in blocks
            ]
            row_counts = [block.shape[2] for block in shaped]
            joined = jnp.concatenate(shaped, axis=2)
            reduced = lax.psum_scatter(joined, axes, scatter_dimension=1, tiled=False)
            cursor = 0
            for branch, count in zip(members, row_counts):
                part = reduced[:, cursor : cursor + count]
                cursor += count
                spread = jax.vmap(lambda block, b=branch: spread_rows(block, strides[b], head_offsets[b]))(
                    part
                )
                total_grad = spread if total_grad is None else total_grad + spread

        return (
            mixed.astype(jnp.bfloat16).reshape(local_rows, model_width),
            query_grad.astype(jnp.bfloat16).reshape(local_rows, model_width),
            total_grad[0].astype(jnp.bfloat16).reshape(local_rows, model_width),
            total_grad[1].astype(jnp.bfloat16).reshape(local_rows, model_width),
        )

    return per_device


def solution(mesh):
    group_count = mesh.shape["groups"]
    seq_devices = mesh.shape["seq"]

    def run(query_rows, key_rows, value_rows, output_grad, head_offsets):
        local_rows = query_rows.shape[0] // (group_count * seq_devices)
        names, sizes, branch_axes = segment_plan(seq_devices, local_rows)
        split_mesh = Mesh(
            mesh.devices.reshape((group_count,) + tuple(sizes)), ("groups",) + tuple(names)
        )
        row_spec = P(("groups",) + tuple(names), None)
        outs = jax.shard_map(
            make_per_device(branch_axes),
            mesh=split_mesh,
            in_specs=(row_spec, row_spec, row_spec, row_spec, P()),
            out_specs=(row_spec, row_spec, row_spec, row_spec),
            check_vma=False,
        )(query_rows, key_rows, value_rows, output_grad, head_offsets)
        placed = NamedSharding(mesh, P(("groups", "seq"), None))
        return tuple(lax.with_sharding_constraint(out, placed) for out in outs)

    return run
```

profile of v0, /device:TPU:0, one launch (start us, length us, event | category | flops | bytes accessed | tf_op | source)
XLA Modules:
  0.0 450.3 jit_solution(16959582659680150816)
XLA Ops:
  7.2 0.0 all-gather.6.cloned.1.call-start
  7.3 1.4 stack.34
  8.6 1.3 stack.31
  9.9 1.3 stack.35
  11.2 1.3 stack.32
  12.4 0.8 slice_bitcast_fusion.18
  13.2 0.4 fusion.18
  13.7 0.5 fusion.17
  14.1 0.8 pad_maximum_fusion.3
  15.0 0.0 all-gather.4.cloned.1.call-start
  15.0 0.2 copy.49
  15.2 0.2 copy.50
  15.4 1.2 compare_bitcast_fusion
  16.6 0.9 maximum_select_fusion.2
  17.4 0.0 all-gather.4.cloned.1.call-update
  17.5 0.0 all-reduce.3.cloned.1.call-start
  17.5 0.2 copy.55
  17.7 0.2 copy.57
  17.9 0.1 broadcast_compare_fusion
  18.0 55.9 %all-gather.6.cloned.1.call-done = bf16[2,640,12,64]{3,2,1,0:T(8,128)(2,1)} async-done(((bf16[2,40,12,64]{3,2,1,0:T(8,128)(2,1)}), bf16[2,640,12,64]{3,2,1,0:T(8,128)(2,1)}) %all-gather.6.cloned.1.call-update) | async-done | bytes 1966096 | tf_op jit(solution)/shard_map/all_gather | solution.py:84
  73.8 3.5 copy.52
  77.4 0.6 slice.64
  78.0 1.0 slice_bitcast_fusion.12
  79.0 2.1 copy.54
  81.1 2.4 copy.53
  83.5 15.2 %all-gather.4.cloned.1.call-done = bf16[2,8,128,12,64]{2,4,3,1,0:T(8,128)(2,1)} async-done(((bf16[2,1,128,12,64]{2,4,3,1,0:T(8,128)(2,1)}), bf16[2,8,128,12,64]{2,4,3,1,0:T(8,128)(2,1)}) %all-gather.4.cloned.1.call-update) | async-done | bytes 3145744 | tf_op jit(solution)/shard_map/all_gather | solution.py:84
  98.8 2.4 copy_bitcast_fusion
  101.2 2.7 pad_maximum_fusion.1
  104.0 15.2 %fusion.22 = (f32[12,128]{1,0:T(8,128)S(1)}, f32[12,128,1664]{1,2,0:T(8,128)}) fusion(bf16[128,12,64]{0,2,1:T(8,128)(2,1)S(1)} %bitcast.129, bf16[2,1664,12,64]{1,3,2,0:T(8,128)(2,1)} %pad_maximum_fusion.1, pred[1664]{0:T(1024)(128)(4,1)S(1)} %copy-done.16, pred[12,128]{1,0:T(8,128)(4,1)S(1)} %get-tuple-element.27, pred[1664]{0:T(1024)(128)(4,1)S(1)} %copy-done.17, ...), kind=kOutput, calls=%fused_computation.58 | convolution fusion | flops 365495936 | bytes 13003776 | tf_op jit(solution)/shard_map/sub | solution.py:114
  119.2 5.1 %fusion.6 = bf16[12,128,1664]{1,2,0:T(8,128)(2,1)S(1)} fusion(f32[12,128,1664]{1,2,0:T(8,128)} %get-tuple-element.25, f32[12,128]{1,0:T(8,128)S(1)} %get-tuple-element.24), kind=kLoop, calls=%fused_computation.18 | loop fusion | flops 5111808 | bytes 15341568 | tf_op jit(solution)/shard_map/convert_element_type | solution.py:117
  124.3 0.2 copy-done.2
  124.5 1.1 multiply_reduce_fusion
  125.7 2.2 convolution_bitcast_fusion
  127.9 7.1 %fusion.1 = bf16[12,128,1664]{1,2,0:T(8,128)(2,1)S(1)} fusion(bf16[128,12,64]{0,2,1:T(8,128)(2,1)S(1)} %bitcast.123, f32[12,128]{1,0:T(8,128)S(1)} %bitcast.133, f32[12,128,1664]{1,2,0:T(8,128)} %get-tuple-element.25, f32[12,128]{1,0:T(8,128)S(1)} %get-tuple-element.24, bf16[2,1664,12,64]{1,3,2,0:T(8,128)(2,1)S(1)} %copy-done.2), kind=kOutput, calls=%fused_computation.6 | convolution fusion | flops 337379328 | bytes 18104320 | tf_op jit(solution)/shard_map/qhe,khe->hqk/dot_general | solution.py:120
  135.0 2.0 multiply_bitcast_fusion
  137.0 0.2 copy-done.3
  137.3 1.0 pad_maximum_fusion.2
  138.3 1.6 copy-done.1
  139.9 0.4 fusion.7
  140.3 2.8 copy.64
  143.1 4.1 copy.63
  147.2 7.3 %pad_maximum_fusion = f32[2,16,40,12,64]{4,2,1,3,0:T(8,128)} fusion(f32[2,16,8,12,64]{4,2,1,3,0:T(8,128)} %bitcast.120, f32[2,16,32,12,64]{4,2,1,3,0:T(8,128)} %bitcast.113), kind=kLoop, calls=%fused_computation.10 | loop fusion | flops 983040 | bytes 7864320 | tf_op jit(solution)/shard_map/concatenate | solution.py:144
  154.5 0.0 reduce-scatter.3.cloned.1.call-start
  154.6 3.4 fusion.3
  158.0 4.2 copy.79
  162.2 9.7 %copy.61 = f32[2,8,128,12,64]{4,2,3,0,1:T(8,128)} copy(f32[2,8,128,12,64]{2,1,4,3,0:T(8,128)} %bitcast.115) | data formatting | bytes 12582912 | tf_op jit(solution)/shard_map/reshape | solution.py:141
  172.0 0.1 copy.65
  172.1 0.1 broadcast_in_dim.143
  172.2 0.1 copy.62
  172.3 0.3 copy-done.14
  172.6 0.6 dynamic-slice
  173.2 4.4 fusion.16
  177.6 0.8 copy.69
  178.4 0.8 copy.68
  179.2 137.1 %all-reduce.3.cloned.1.call-done = f32[2,16,40,12,64]{4,2,1,3,0:T(8,128)} async-done(((f32[2,16,40,12,64]{4,2,1,3,0:T(8,128)}), f32[2,16,40,12,64]{4,2,1,3,0:T(8,128)}) %all-reduce.3.cloned.1.call-update) | async-done | bytes 3932176
  316.4 1.7 dynamic-slice_bitcast_fusion
  318.1 121.4 %reduce-scatter.3.cloned.1.call-done = f32[2,1,128,12,64]{4,2,3,0,1:T(8,128)} async-done(((f32[2,8,128,12,64]{4,2,3,0,1:T(8,128)}), f32[2,1,128,12,64]{4,2,3,0,1:T(8,128)}) %reduce-scatter.3.cloned.1.call-update) | async-done | bytes 786448 | tf_op jit(solution)/shard_map/reduce_scatter | solution.py:145
  439.5 0.3 broadcast_in_dim.140
  439.8 1.8 fusion.12
  441.6 0.1 fusion.21
  441.7 0.2 copy.67
  441.9 0.8 copy.71
  442.7 0.2 copy.66
  442.9 0.8 copy.70
  (45 shorter events, 0.2 us)
Async XLA Ops:
  7.2 7.9 %copy-start.5 = (bf16[128,768]{1,0:T(8,128)(2,1)S(1)}, bf16[128,768]{1,0:T(8,128)(2,1)}, u32[]{:S(2)}) copy-start(bf16[128,768]{1,0:T(8,128)(2,1)} %param.9) | copy-start | bytes 589828
  7.2 8.0 %copy-start.6 = (bf16[128,768]{1,0:T(8,128)(2,1)S(1)}, bf16[128,768]{1,0:T(8,128)(2,1)}, u32[]{:S(2)}) copy-start(bf16[128,768]{1,0:T(8,128)(2,1)} %param.10) | copy-start | bytes 589828
  7.2 10.3 %copy-start.10 = (bf16[128,768]{1,0:T(8,128)(2,1)S(1)}, bf16[128,768]{1,0:T(8,128)(2,1)}, u32[]{:S(2)}) copy-start(bf16[128,768]{1,0:T(8,128)(2,1)} %param.8) | copy-start | bytes 589828
  7.2 10.5 %copy-start.11 = (bf16[128,768]{1,0:T(8,128)(2,1)S(1)}, bf16[128,768]{1,0:T(8,128)(2,1)}, u32[]{:S(2)}) copy-start(bf16[128,768]{1,0:T(8,128)(2,1)} %param.11) | copy-start | bytes 589828
  7.2 66.6 %all-gather.6.cloned.1.call-start = ((), (), s32[]{:S(2)}) async-start(), calls=%async_computation.3 | async-start | bytes 5570560 | tf_op jit(solution)/shard_map/all_gather | solution.py:84
  15.0 83.8 %all-gather.4.cloned.1.call-start = ((), (), s32[]{:S(2)}) async-start(), calls=%async_computation.1 | async-start | bytes 3538944 | tf_op jit(solution)/shard_map/all_gather | solution.py:84
  16.6 60.8 %copy-start.12 = (pred[12]{0:T(512)(128)(4,1)}, pred[12]{0:T(512)(128)(4,1)S(1)}, u32[]{:S(2)}) copy-start(pred[12]{0:T(512)(128)(4,1)S(1)} %get-tuple-element.21) | copy-start | bytes 40
  17.5 298.9 %all-reduce.3.cloned.1.call-start = ((), (), s32[]{:S(2)}) async-start(), calls=%async_computation.4 | async-start | bytes 15728640
  17.7 86.3 %copy-start.8 = (bf16[128,768]{0,1:T(8,128)(2,1)}, bf16[128,768]{0,1:T(8,128)(2,1)S(1)}, u32[]{:S(2)}) copy-start(bf16[128,768]{0,1:T(8,128)(2,1)S(1)} %copy.55) | copy-start | bytes 589828
  83.5 17.6 %copy-start.4 = (bf16[2,512,12,64]{1,3,2,0:T(8,128)(2,1)S(1)}, bf16[2,512,12,64]{1,3,2,0:T(8,128)(2,1)}, u32[]{:S(2)}) copy-start(bf16[2,512,12,64]{1,3,2,0:T(8,128)(2,1)} %copy.53) | copy-start | bytes 4718596
  83.5 17.6 %copy-start.7 = (bf16[2,128,12,64]{1,3,2,0:T(8,128)(2,1)S(1)}, bf16[2,128,12,64]{1,3,2,0:T(8,128)(2,1)}, u32[]{:S(2)}) copy-start(bf16[2,128,12,64]{1,3,2,0:T(8,128)(2,1)} %copy.54) | copy-start | bytes 1179652
  101.2 2.8 copy-start.15
  101.2 2.8 copy-start.16
  101.2 2.8 copy-start.17
  101.2 2.8 copy-start.18
  119.2 5.4 %copy-start.2 = (bf16[2,1664,12,64]{1,3,2,0:T(8,128)(2,1)S(1)}, bf16[2,1664,12,64]{1,3,2,0:T(8,128)(2,1)}, u32[]{:S(2)}) copy-start(bf16[2,1664,12,64]{1,3,2,0:T(8,128)(2,1)} %pad_maximum_fusion.1) | copy-start | bytes 15335428
  127.9 10.4 %copy-start = (f32[1,1664,12,64]{1,3,2,0:T(8,128)}, f32[1,1664,12,64]{1,3,2,0:T(8,128)S(1)}, u32[]{:S(2)}) copy-start(f32[1,1664,12,64]{1,3,2,0:T(8,128)S(1)} %convolution_bitcast_fusion) | copy-start | bytes 15335428
  127.9 7.2 %copy-start.9 = (bf16[128,768]{0,1:T(8,128)(2,1)S(1)}, bf16[128,768]{0,1:T(8,128)(2,1)}, u32[]{:S(2)}) copy-start(bf16[128,768]{0,1:T(8,128)(2,1)} %copy-done.8) | copy-start | bytes 589828
  135.0 2.2 copy-start.3
  137.3 2.6 copy-start.1
  154.5 285.0 %reduce-scatter.3.cloned.1.call-start = ((), (), s32[]{:S(2)}) async-start(), calls=%async_computation.2 | async-start | bytes 14155776 | tf_op jit(solution)/shard_map/reduce_scatter | solution.py:145
  171.9 0.7 copy-start.14
  173.2 266.6 %copy-start.13 = (pred[12]{0:T(512)(128)(4,1)S(1)}, pred[12]{0:T(512)(128)(4,1)}, u32[]{:S(2)}) copy-start(pred[12]{0:T(512)(128)(4,1)} %copy-done.12) | copy-start | bytes 40
Sparse Core Ops, SparseCore 0:
  15.1 58.6 all-gather.5
  75.4 23.2 all-gather.3
  154.6 161.6 all-reduce.2
  318.6 120.8 reduce-scatter.2
where the time goes:
time: 458 us; the launch traced here: 450 us
  waiting for transfers between devices  330 us (72%)
  local copies, waits for them, and re-layouts  48.5 us (11%)
  matrix products  32 us (7%)
  other arithmetic  25.7 us (6%)
  between operations  14.2 us (3%)
    unnamed x5, waiting for transfers between devices  137 us
    reduce_scatter x1, waiting for transfers between devices, per_device(): reduced = lax.psum_scatter(joined, axes, scatter_dimension=1, tiled=False)  121 us
    all_gather x2, waiting for transfers between devices, per_device(): full = lax.all_gather(joined, axes, axis=1, tiled=False)  71.1 us
    sub x1, matrix products, per_device(): expo = jnp.where(valid, jnp.exp(scores - peak), 0.0)  15.2 us
    unnamed x48, local copies, waits for them, and re-layouts  11.2 us
    reshape x1, local copies, waits for them, and re-layouts, per_device(): block.reshape(2, dev_count, -1, head_count, head_dim)  9.74 us
  transfers between devices with their start and end apart: 4, of which 4 were waited for; matrix products, arithmetic and copies ran while one was open for 9% of the time, Pallas kernels for 0%

commit v1 on v0

v1 whole, which is shorter than its diff:
```python
import math

import numpy as np
import jax
import jax.numpy as jnp
from jax import lax
from jax.sharding import PartitionSpec as P

LEN_NEAR = 1024
LEN_MID = 4096
LEN_FAR = 16384
DILATION_FIRST = 1
DILATION_SECOND = 4
DILATION_THIRD = 16

NEG_FILL = -1e30


def exchange(block, bit):
    count = lax.axis_size("seq")
    route = [(index, index ^ (1 << bit)) for index in range(count)]
    return lax.ppermute(block, "seq", route)


def pick_rows(rows, stride, offsets_row):
    count = rows.shape[0]
    grouped = rows.reshape((count // stride, stride) + rows.shape[1:])
    chosen = (jnp.arange(stride, dtype=jnp.int32)[:, None] == offsets_row[None, :])[
        None, :, None, :, None
    ]
    return jnp.sum(jnp.where(chosen, grouped, jnp.zeros((), rows.dtype)), axis=1)


def spread_rows(picked, stride, offsets_row):
    count = picked.shape[0]
    chosen = (jnp.arange(stride, dtype=jnp.int32)[:, None] == offsets_row[None, :])[
        None, :, None, :, None
    ]
    widened = jnp.where(chosen, picked[:, None], jnp.zeros((), picked.dtype))
    return widened.reshape((count * stride,) + picked.shape[1:])


def make_per_device(branch_bits):
    strides = [DILATION_FIRST, DILATION_SECOND, DILATION_THIRD]
    top_bits = max(branch_bits)

    def per_device(query_rows, key_rows, value_rows, output_grad, head_offsets):
        local_rows, model_width = query_rows.shape
        head_count = head_offsets.shape[1]
        head_dim = model_width // head_count
        score_scale = 1.0 / math.sqrt(head_dim)
        shape3 = (local_rows, head_count, head_dim)
        query3 = query_rows.reshape(shape3)
        key3 = key_rows.reshape(shape3)
        value3 = value_rows.reshape(shape3)
        grad3 = output_grad.reshape(shape3)
        kv3 = jnp.stack([key3, value3], axis=1)

        buffers = [
            pick_rows(kv3, strides[branch], head_offsets[branch]) for branch in range(3)
        ]
        for bit in reversed(range(top_bits)):
            active = [branch for branch in range(3) if branch_bits[branch] > bit]
            outgoing = jnp.concatenate([buffers[branch].reshape(-1) for branch in active])
            incoming = exchange(outgoing, bit)
            cursor = 0
            for branch in active:
                size = buffers[branch].size
                arrived = incoming[cursor : cursor + size].reshape(buffers[branch].shape)
                cursor += size
                buffers[branch] = jnp.stack([buffers[branch], arrived])
        gathered = [
            buffers[branch].reshape((-1,) + kv3.shape[1:]) for branch in range(3)
        ]
        key_counts = [block.shape[0] for block in gathered]
        kv_all = jnp.concatenate(gathered, axis=0)
        key_all = kv_all[:, 0]
        value_all = kv_all[:, 1]

        local_index = jnp.arange(local_rows, dtype=jnp.int32)
        member = [
            (local_index[None, :] % strides[branch]) == head_offsets[branch][:, None]
            for branch in range(3)
        ]
        key_branch = np.concatenate(
            [np.full((count,), branch, np.int32) for branch, count in enumerate(key_counts)]
        )
        valid = None
        for branch in range(3):
            term = member[branch][:, :, None] & jnp.asarray(key_branch == branch)[None, None, :]
            valid = term if valid is None else valid | term

        scores = (
            jnp.einsum("qhe,khe->hqk", query3, key_all, preferred_element_type=jnp.float32)
            * score_scale
        )
        scores = jnp.where(valid, scores, NEG_FILL)
        peak = jnp.max(scores, axis=2, keepdims=True)
        expo = jnp.where(valid, jnp.exp(scores - peak), 0.0)
        total = jnp.sum(expo, axis=2, keepdims=True)
        prob = expo / total
        weight = prob.astype(jnp.bfloat16)
        mixed = jnp.einsum("hqk,khe->qhe", weight, value_all, preferred_element_type=jnp.float32)
        balance = jnp.sum(grad3.astype(jnp.float32) * mixed, axis=2)
        flow = jnp.einsum("qhe,khe->hqk", grad3, value_all, preferred_element_type=jnp.float32)
        score_grad = (prob * (flow - jnp.transpose(balance)[:, :, None])).astype(jnp.bfloat16)
        query_grad = (
            jnp.einsum("hqk,khe->qhe", score_grad, key_all, preferred_element_type=jnp.float32)
            * score_scale
        )
        key_terms = (
            jnp.einsum("hqk,qhe->khe", score_grad, query3, preferred_element_type=jnp.float32)
            * score_scale
        )
        value_terms = jnp.einsum("hqk,qhe->khe", weight, grad3, preferred_element_type=jnp.float32)
        terms = jnp.stack([key_terms, value_terms], axis=1)

        starts = np.cumsum([0] + key_counts)
        partial = []
        for branch in range(3):
            block = terms[starts[branch] : starts[branch + 1]]
            partial.append(block.reshape((2,) * branch_bits[branch] + (-1,) + terms.shape[1:]))
        for bit in range(top_bits):
            active = [branch for branch in range(3) if branch_bits[branch] > bit]
            outgoing = jnp.concatenate([partial[branch][1].reshape(-1) for branch in active])
            incoming = exchange(outgoing, bit)
            cursor = 0
            for branch in active:
                kept = partial[branch][0]
                size = kept.size
                partial[branch] = kept + incoming[cursor : cursor + size].reshape(kept.shape)
                cursor += size
        total_grad = None
        for branch in range(3):
            spread = spread_rows(partial[branch], strides[branch], head_offsets[branch])
            total_grad = spread if total_grad is None else total_grad + spread

        return (
            mixed.astype(jnp.bfloat16).reshape(local_rows, model_width),
            query_grad.astype(jnp.bfloat16).reshape(local_rows, model_width),
            total_grad[:, 0].astype(jnp.bfloat16).reshape(local_rows, model_width),
            total_grad[:, 1].astype(jnp.bfloat16).reshape(local_rows, model_width),
        )

    return per_device


def solution(mesh):
    group_count = mesh.shape["groups"]
    seq_devices = mesh.shape["seq"]

    def run(query_rows, key_rows, value_rows, output_grad, head_offsets):
        local_rows = query_rows.shape[0] // (group_count * seq_devices)
        tokens_all = seq_devices * local_rows
        seg_lengths = [min(LEN_NEAR, tokens_all), min(LEN_MID, tokens_all), min(LEN_FAR, tokens_all)]
        branch_bits = [(seg_length // local_rows).bit_length() - 1 for seg_length in seg_lengths]
        row_spec = P(("groups", "seq"), None)
        return jax.shard_map(
            make_per_device(branch_bits),
            mesh=mesh,
            in_specs=(row_spec, row_spec, row_spec, row_spec, P()),
            out_specs=(row_spec, row_spec, row_spec, row_spec),
            check_vma=False,
        )(query_rows, key_rows, value_rows, output_grad, head_offsets)

    return run
```

time: 458 us -> 444 us (0.969)
  waiting for transfers between devices: 330 us -> 134 us
  local copies, waits for them, and re-layouts: 48.5 us -> 184 us
  other arithmetic: 25.7 us -> 70.6 us
  starting transfers between devices: 0.16 us -> 13.7 us
  between operations: 14.2 us -> 1.94 us
    unnamed x5 -> x0, waiting for transfers between devices: 137 us -> none
    ppermute x0 -> x8, waiting for transfers between devices: none -> 134 us  [exchange(): return lax.ppermute(block, 'seq', route)]
    reduce_scatter x1 -> x0, waiting for transfers between devices: 121 us -> none  [per_device(): reduced = lax.psum_scatter(joined, axes, scatter_dimension=1, tiled=False)]
    all_gather x2 -> x0, waiting for transfers between devices: 71.1 us -> none  [per_device(): full = lax.all_gather(joined, axes, axis=1, tiled=False)]
    another operation x4 -> x48, local copies, waits for them, and re-layouts: 5.15 us -> 59.7 us  [the longest x33 35.2 us: per_device(): buffers[branch] = jnp.stack([buffers[branch], arrived])]
    slice x8 -> x48, local copies, waits for them, and re-layouts: 7.94 us -> 48.7 us  [the longest x19 27 us: per_device(): partial[branch][1].reshape(-1)]
    reshape x5 -> x27, local copies, waits for them, and re-layouts: 17.7 us -> 48.9 us  [the longest x14 31 us: per_device(): partial[branch] = kept + incoming[cursor:cursor + size].reshape(kept.shape)]
    add x0 -> x10, other arithmetic: none -> 17.3 us  [per_device(): partial[branch] = kept + incoming[cursor:cursor + size].reshape(kept.shape)]
  transfers between devices with their start and end apart: 4 -> 8, of which waited for: 4 -> 7; matrix products, arithmetic and copies ran while one was open for 9% -> 5% of each run, Pallas kernels for 0% -> 0%
where the time goes in v1:
time: 444 us; the launch traced here: 436 us
  local copies, waits for them, and re-layouts  184 us (41%)
  waiting for transfers between devices  134 us (30%)
  other arithmetic  70.6 us (16%)
  matrix products  30.8 us (7%)
  starting transfers between devices  13.7 us (3%)
    ppermute x8, waiting for transfers between devices, exchange(): return lax.ppermute(block, 'seq', route)  134 us
    another operation x33, local copies, waits for them, and re-layouts, per_device(): buffers[branch] = jnp.stack([buffers[branch], arrived])  35.2 us
    reshape x14, local copies, waits for them, and re-layouts, per_device(): partial[branch] = kept + incoming[cursor:cursor + size].reshape(kept.shape)  31 us
    slice x19, local copies, waits for them, and re-layouts, per_device(): partial[branch][1].reshape(-1)  27 us
    another operation x11, local copies, waits for them, and re-layouts, per_device(): partial[branch][1].reshape(-1)  19.4 us
    add x10, other arithmetic, per_device(): partial[branch] = kept + incoming[cursor:cursor + size].reshape(kept.shape)  17.3 us
    unnamed x88, local copies, waits for them, and re-layouts  16.9 us
    sub x1, matrix products, per_device(): expo = jnp.where(valid, jnp.exp(scores - peak), 0.0)  15.2 us
  transfers between devices with their start and end apart: 8, of which 7 were waited for; matrix products, arithmetic and copies ran while one was open for 5% of the time, Pallas kernels for 0%

profile of v1, /device:TPU:0, one launch (start us, length us, event | category | flops | bytes accessed | tf_op | source)
XLA Modules:
  0.0 435.7 jit_solution(18171380985233491908)
XLA Ops:
  8.0 4.1 collective-permute-start
  15.7 2.3 collective-permute-done
  20.1 14.7 %collective-permute-done.1 = bf16[319488]{0:T(1024)(128)(2,1)S(1)} collective-permute-done((bf16[319488]{0:T(1024)(128)(2,1)S(1)}, bf16[319488]{0:T(1024)(128)(2,1)S(1)}, u32[]{:S(2)}, u32[]{:S(2)}) %collective-permute-start.1) | collective-permute-done | bytes 639008 | tf_op jit(solution)/shard_map/ppermute | solution.py:22
  40.6 4.1 copy.113
  44.6 1.8 reshape.449
  49.0 27.1 %collective-permute-done.2 = bf16[638976]{0:T(1024)(128)(2,1)S(1)} collective-permute-done((bf16[638976]{0:T(1024)(128)(2,1)S(1)}, bf16[638976]{0:T(1024)(128)(2,1)S(1)}, u32[]{:S(2)}, u32[]{:S(2)}) %collective-permute-start.2) | collective-permute-done | bytes 1277984 | tf_op jit(solution)/shard_map/ppermute | solution.py:22
  81.7 1.8 reshape.453
  83.5 2.1 slice.312
  85.6 2.6 stack_reshape.40
  88.2 2.5 copy.118
  90.8 2.5 fusion.40
  93.3 6.5 %copy.119 = bf16[2,2,128,2,12,64]{5,4,3,2,1,0:T(8,128)(2,1)} copy(bf16[2,2,128,2,12,64]{2,5,4,3,1,0:T(8,128)(2,1)S(1)} %get-tuple-element.23) | data formatting | bytes 3145728 | tf_op jit(solution)/shard_map/stack | solution.py:71
  99.8 4.9 %reshape.452 = bf16[786432]{0:T(1024)(128)(2,1)S(1)} reshape(bf16[2,2,128,2,12,64]{5,4,3,2,1,0:T(8,128)(2,1)} %copy.119) | data formatting | bytes 3145728 | tf_op jit(solution)/shard_map/reshape | solution.py:64
  104.7 13.7 %pad_maximum_fusion.4 = bf16[1277952]{0:T(1024)(128)(2,1)} fusion(bf16[98304]{0:T(1024)(128)(2,1)S(1)} %reshape.454, bf16[393216]{0:T(1024)(128)(2,1)S(1)} %copy-done.15, bf16[786432]{0:T(1024)(128)(2,1)S(1)} %reshape.452), kind=kLoop, calls=%fused_computation.33 | loop fusion | flops 7667712 | bytes 5111808 | tf_op jit(solution)/shard_map/concatenate | solution.py:64
  119.5 3.9 collective-permute-done.3
  130.8 2.4 copy.130
  134.6 3.4 stack_reshape.43
  137.9 5.1 %copy.124 = bf16[1,2,2,128,2,12,64]{3,6,5,4,2,1,0:T(8,128)(2,1)S(1)} copy(bf16[1,2,2,128,2,12,64]{6,5,4,3,2,1,0:T(8,128)(2,1)} %stack_reshape.43) | data formatting | bytes 3145728 | tf_op jit(solution)/shard_map/stack;reshape | solution.py:71
  143.4 3.2 copy.125
  146.6 3.9 reshape.455
  150.6 5.9 %pad_maximum_fusion = bf16[1664,2,12,64]{0,3,2,1:T(8,128)(2,1)} fusion(bf16[128,2,12,64]{0,3,2,1:T(8,128)(2,1)} %copy.131, bf16[512,2,12,64]{0,3,2,1:T(8,128)(2,1)} %copy.130, bf16[1024,2,12,64]{0,3,2,1:T(8,128)(2,1)} %reshape.455), kind=kLoop, calls=%fused_computation.17 | loop fusion | flops 15335424 | bytes 10223616 | tf_op jit(solution)/shard_map/concatenate | solution.py:76
  156.5 15.2 %fusion.42 = (f32[12,128]{1,0:T(8,128)S(1)}, f32[12,128,1664]{1,2,0:T(8,128)}) fusion(bf16[128,12,64]{0,2,1:T(8,128)(2,1)S(1)} %bitcast.168, bf16[1664,2,12,64]{0,3,2,1:T(8,128)(2,1)} %pad_maximum_fusion, pred[1664]{0:T(1024)(128)(4,1)S(1)} %copy-done.37, pred[12,128]{1,0:T(8,128)(4,1)S(1)} %get-tuple-element.49, pred[1664]{0:T(1024)(128)(4,1)S(1)} %copy-done.38, ...), kind=kOutput, calls=%fused_computation.110 | convolution fusion | flops 365495936 | bytes 13003776 | tf_op jit(solution)/shard_map/sub | solution.py:99
  171.7 5.1 %fusion.5 = bf16[12,128,1664]{1,2,0:T(8,128)(2,1)S(1)} fusion(f32[12,128,1664]{1,2,0:T(8,128)} %get-tuple-element.47, f32[12,128]{1,0:T(8,128)S(1)} %get-tuple-element.46), kind=kLoop, calls=%fused_computation.23 | loop fusion | flops 5111808 | bytes 15341568 | tf_op jit(solution)/shard_map/convert_element_type | solution.py:102
  177.1 1.8 multiply_reduce_fusion
  178.9 2.2 convolution_bitcast_fusion
  181.1 5.3 %fusion.1 = bf16[12,128,1664]{1,2,0:T(8,128)(2,1)S(1)} fusion(bf16[128,12,64]{0,2,1:T(8,128)(2,1)S(1)} %bitcast.163, f32[12,128]{1,0:T(8,128)S(1)} %bitcast.173, f32[12,128,1664]{1,2,0:T(8,128)} %get-tuple-element.47, f32[12,128]{1,0:T(8,128)S(1)} %get-tuple-element.46, bf16[1664,2,12,64]{0,3,2,1:T(8,128)(2,1)S(1)} %copy-done), kind=kOutput, calls=%fused_computation.12 | convolution fusion | flops 337379328 | bytes 18104320 | tf_op jit(solution)/shard_map/qhe,khe->hqk/dot_general | solution.py:105
  186.4 2.0 multiply_bitcast_fusion
  190.1 2.1 fusion.11
  192.2 2.5 fusion.6
  194.7 2.9 copy.140
  198.9 5.5 %copy.139 = f32[256,2,12,64]{3,2,1,0:T(8,128)} copy(f32[256,2,12,64]{0,3,2,1:T(8,128)} %get-tuple-element.19) | data formatting | bytes 3145728 | tf_op jit(solution)/shard_map/slice | solution.py:125
  204.4 4.3 reshape_squeeze.34
  208.8 7.8 %copy.138 = f32[512,2,12,64]{3,2,1,0:T(8,128)} copy(f32[512,2,12,64]{0,3,2,1:T(8,128)S(1)} %get-tuple-element.17) | data formatting | bytes 6291456 | tf_op jit(solution)/shard_map/slice | solution.py:125
  216.6 5.2 %reshape_squeeze.33 = f32[786432]{0:T(1024)S(1)} reshape(f32[512,2,12,64]{3,2,1,0:T(8,128)} %copy.138) | data formatting | bytes 6291456 | tf_op jit(solution)/shard_map/reshape;squeeze | solution.py:125
  221.8 5.1 %pad_maximum_fusion.1 = f32[1277952]{0:T(1024)} fusion(f32[98304]{0:T(1024)S(1)} %reshape_squeeze.35, f32[393216]{0:T(1024)} %reshape_squeeze.34, f32[786432]{0:T(1024)S(1)} %reshape_squeeze.33), kind=kLoop, calls=%fused_computation.18 | loop fusion | flops 2555904 | bytes 10223616 | tf_op jit(solution)/shard_map/concatenate | solution.py:125
  227.1 2.3 copy.147
  229.4 3.4 copy.144
  232.7 4.2 squeeze.43
  239.2 1.9 copy_add_fusion.2
  244.2 2.7 slice.333
  246.9 3.9 reshape.463
  250.8 5.0 %copy_add_fusion = f32[2,2,2,32,2,12,64]{6,3,2,1,0,5,4:T(8,128)S(1)} fusion(f32[2,2,2,32,2,12,64]{6,3,2,1,0,5,4:T(8,128)} %bitcast.152, f32[2,2,2,32,2,12,64]{6,5,4,3,2,1,0:T(8,128)} %reshape.463), kind=kLoop, calls=%fused_computation.29 | loop fusion | flops 393216 | bytes 4718592 | tf_op jit(solution)/shard_map/add | solution.py:131
  257.7 2.3 copy.146
  260.0 2.5 reshape_squeeze.37
  262.5 3.8 slice.328
  266.3 6.5 %reshape.462 = f32[2,2,128,2,12,64]{5,4,3,2,1,0:T(8,128)} reshape(f32[786432]{0:T(1024)} %slice.328) | data formatting | bytes 6291456 | tf_op jit(solution)/shard_map/reshape | solution.py:131
  272.8 7.1 %copy.142 = f32[2,2,128,2,12,64]{2,5,4,3,1,0:T(8,128)} copy(f32[2,2,128,2,12,64]{5,4,3,2,1,0:T(8,128)} %reshape.462) | data formatting | bytes 6291456 | tf_op jit(solution)/shard_map/reshape | solution.py:131
  279.9 2.7 copy_add_fusion.1
  284.3 4.5 %copy.143 = f32[1,2,128,2,12,64]{5,4,3,2,1,0:T(8,128)} copy(f32[1,2,128,2,12,64]{2,5,4,3,1,0:T(8,128)S(1)} %slice.330) | data formatting | bytes 3145728 | tf_op jit(solution)/shard_map/slice | solution.py:125
  288.8 3.2 reshape_squeeze.36
  293.6 56.4 %collective-permute-done.5 = f32[638976]{0:T(1024)S(1)} collective-permute-done((f32[638976]{0:T(1024)S(1)}, f32[638976]{0:T(1024)S(1)}, u32[]{:S(2)}, u32[]{:S(2)}) %collective-permute-start.5) | collective-permute-done | bytes 2555936 | tf_op jit(solution)/shard_map/ppermute | solution.py:22
  353.6 2.2 slice.341
  355.8 2.7 reshape.466
  358.5 2.5 fusion.13
  363.7 2.5 reshape.465
  366.2 4.4 %copy.150 = f32[2,128,2,12,64]{1,4,3,2,0:T(8,128)} copy(f32[2,128,2,12,64]{4,3,2,1,0:T(8,128)} %reshape.465) | data formatting | bytes 3145728 | tf_op jit(solution)/shard_map/reshape | solution.py:131
  373.5 1.8 copy.151
  376.8 2.3 collective-permute-start.6
  379.4 27.7 %collective-permute-done.6 = f32[319488]{0:T(1024)S(1)} collective-permute-done((f32[319488]{0:T(1024)}, f32[319488]{0:T(1024)S(1)}, u32[]{:S(2)}, u32[]{:S(2)}) %collective-permute-start.6) | collective-permute-done | bytes 1277984 | tf_op jit(solution)/shard_map/ppermute | solution.py:22
  411.3 3.7 collective-permute-start.7
  415.0 4.3 fusion.17
  421.4 1.9 copy.156
  423.3 2.1 collective-permute-done.7
  431.8 2.0 fusion.26
  (231 shorter events, 75.6 us)
Async XLA Ops:
  1.9 10.3 %copy-start.21 = (bf16[128,768]{1,0:T(8,128)(2,1)S(1)}, bf16[128,768]{1,0:T(8,128)(2,1)}, u32[]{:S(2)}) copy-start(bf16[128,768]{1,0:T(8,128)(2,1)} %param.10) | copy-start | bytes 589828
  3.2 9.1 %copy-start.22 = (bf16[128,768]{1,0:T(8,128)(2,1)S(1)}, bf16[128,768]{1,0:T(8,128)(2,1)}, u32[]{:S(2)}) copy-start(bf16[128,768]{1,0:T(8,128)(2,1)} %param.9) | copy-start | bytes 589828
  6.6 0.6 copy-start.30
  7.3 8.4 %copy-start.34 = (pred[4,12]{1,0:T(4,128)(4,1)}, pred[4,12]{1,0:T(4,128)(4,1)S(1)}, u32[]{:S(2)}) copy-start(pred[4,12]{1,0:T(4,128)(4,1)S(1)} %iota_compare_fusion.1) | copy-start | bytes 148
  8.0 10.1 %collective-permute-start = (bf16[61440]{0:T(1024)(128)(2,1)S(1)}, bf16[61440]{0:T(1024)(128)(2,1)S(1)}, u32[]{:S(2)}, u32[]{:S(2)}) collective-permute-start(bf16[61440]{0:T(1024)(128)(2,1)S(1)} %pad_maximum_fusion.19), channel_id=1, source_target_pairs={{0,8},{1,9},{2,10},{3,11},{4,12},{5,13},{6,14},{7,15},{8,0},{9,1},... | collective-permute-start | bytes 368648 | tf_op jit(solution)/shard_map/ppermute | solution.py:22
  13.7 6.3 %copy-start.32 = (pred[12]{0:T(512)(128)(4,1)}, pred[12]{0:T(512)(128)(4,1)S(1)}, u32[]{:S(2)}) copy-start(pred[12]{0:T(512)(128)(4,1)S(1)} %get-tuple-element.43) | copy-start | bytes 40
  19.2 15.6 %collective-permute-start.1 = (bf16[319488]{0:T(1024)(128)(2,1)S(1)}, bf16[319488]{0:T(1024)(128)(2,1)S(1)}, u32[]{:S(2)}, u32[]{:S(2)}) collective-permute-start(bf16[319488]{0:T(1024)(128)(2,1)S(1)} %pad_maximum_fusion.14), channel_id=1, source_target_pairs={{0,4},{1,5},{2,6},{3,7},{4,0},{5,1},{6,2},{7,3},{8,12},{9,13},{10,... | collective-permute-start | bytes 1916936 | tf_op jit(solution)/shard_map/ppermute | solution.py:22
  47.7 28.4 %collective-permute-start.2 = (bf16[638976]{0:T(1024)(128)(2,1)S(1)}, bf16[638976]{0:T(1024)(128)(2,1)S(1)}, u32[]{:S(2)}, u32[]{:S(2)}) collective-permute-start(bf16[638976]{0:T(1024)(128)(2,1)S(1)} %pad_maximum_fusion.8), channel_id=1, source_target_pairs={{0,2},{1,3},{2,0},{3,1},{4,6},{5,7},{6,4},{7,5},{8,10},{9,11},{10,... | collective-permute-start | bytes 3833864 | tf_op jit(solution)/shard_map/ppermute | solution.py:22
  76.1 1.1 copy-start.23
  77.2 1.5 slice-start.3
  78.3 1.1 copy-start.14
  99.7 4.9 %copy-start.15 = (bf16[393216]{0:T(1024)(128)(2,1)S(1)}, bf16[393216]{0:T(1024)(128)(2,1)}, u32[]{:S(2)}) copy-start(bf16[393216]{0:T(1024)(128)(2,1)} %reshape.453) | copy-start | bytes 2359300
  104.7 13.8 %copy-start.28 = (bf16[128,768]{1,0:T(8,128)(2,1)S(1)}, bf16[128,768]{1,0:T(8,128)(2,1)}, u32[]{:S(2)}) copy-start(bf16[128,768]{1,0:T(8,128)(2,1)} %param.11) | copy-start | bytes 589828
  104.7 13.9 %copy-start.29 = (bf16[128,768]{1,0:T(8,128)(2,1)S(1)}, bf16[128,768]{1,0:T(8,128)(2,1)}, u32[]{:S(2)}) copy-start(bf16[128,768]{1,0:T(8,128)(2,1)} %param.8) | copy-start | bytes 589828
  118.4 5.0 %collective-permute-start.3 = (bf16[1277952]{0:T(1024)(128)(2,1)}, bf16[1277952]{0:T(1024)(128)(2,1)S(1)}, u32[]{:S(2)}, u32[]{:S(2)}) collective-permute-start(bf16[1277952]{0:T(1024)(128)(2,1)} %pad_maximum_fusion.4), channel_id=1, source_target_pairs={{0,1},{1,0},{2,3},{3,2},{4,5},{5,4},{6,7},{7,6},{8,9},{9,8},{10,11... | collective-permute-start | bytes 7667720 | tf_op jit(solution)/shard_map/ppermute | solution.py:22
  123.4 3.2 copy-start.6
  127.6 1.4 copy-start.10
  133.2 1.4 slice-start
  137.9 5.1 %copy-start.11 = (bf16[1,2,2,128,2,12,64]{3,6,5,4,2,1,0:T(8,128)(2,1)S(1)}, bf16[1,2,2,128,2,12,64]{3,6,5,4,2,1,0:T(8,128)(2,1)}, u32[]{:S(2)}) copy-start(bf16[1,2,2,128,2,12,64]{3,6,5,4,2,1,0:T(8,128)(2,1)} %get-tuple-element.22) | copy-start | bytes 4718596
  150.5 6.0 %copy-start.26 = (bf16[128,768]{0,1:T(8,128)(2,1)S(1)}, bf16[128,768]{0,1:T(8,128)(2,1)}, u32[]{:S(2)}) copy-start(bf16[128,768]{0,1:T(8,128)(2,1)} %copy.132) | copy-start | bytes 589828
  150.5 6.0 %copy-start.36 = (pred[12]{0:T(512)(128)(4,1)S(1)}, pred[12]{0:T(512)(128)(4,1)}, u32[]{:S(2)}) copy-start(pred[12]{0:T(512)(128)(4,1)} %get-tuple-element.42) | copy-start | bytes 40
  150.5 6.0 %copy-start.37 = (pred[1664]{0:T(1024)(128)(4,1)S(1)}, pred[1664]{0:T(1024)(128)(4,1)}, u32[]{:S(2)}) copy-start(pred[1664]{0:T(1024)(128)(4,1)} %constant.61.clone) | copy-start | bytes 4996
  150.5 6.0 %copy-start.38 = (pred[1664]{0:T(1024)(128)(4,1)S(1)}, pred[1664]{0:T(1024)(128)(4,1)}, u32[]{:S(2)}) copy-start(pred[1664]{0:T(1024)(128)(4,1)} %constant.60.clone) | copy-start | bytes 4996
  150.5 6.0 %copy-start.39 = (pred[1664]{0:T(1024)(128)(4,1)S(1)}, pred[1664]{0:T(1024)(128)(4,1)}, u32[]{:S(2)}) copy-start(pred[1664]{0:T(1024)(128)(4,1)} %constant.59.clone) | copy-start | bytes 4996
  171.7 5.4 %copy-start = (bf16[1664,2,12,64]{0,3,2,1:T(8,128)(2,1)S(1)}, bf16[1664,2,12,64]{0,3,2,1:T(8,128)(2,1)}, u32[]{:S(2)}) copy-start(bf16[1664,2,12,64]{0,3,2,1:T(8,128)(2,1)} %pad_maximum_fusion) | copy-start | bytes 15335428
  186.4 2.2 copy-start.1
  226.9 10.0 %collective-permute-start.4 = (f32[1277952]{0:T(1024)}, f32[1277952]{0:T(1024)}, u32[]{:S(2)}, u32[]{:S(2)}) collective-permute-start(f32[1277952]{0:T(1024)} %pad_maximum_fusion.1), channel_id=1, source_target_pairs={{0,1},{1,0},{2,3},{3,2},{4,5},{5,4},{6,7},{7,6},{8,9},{9,8},{10,11... | collective-permute-start | bytes 15335432 | tf_op jit(solution)/shard_map/ppermute | solution.py:22
  241.1 0.9 copy-start.18
  255.8 1.7 copy-start.2
  282.6 1.6 copy-start.4
  288.8 3.2 copy-start.16
  292.1 59.7 %copy-start.19 = (f32[2,2,2,8,2,12,64]{6,3,2,1,0,5,4:T(8,128)S(1)}, f32[2,2,2,8,2,12,64]{6,3,2,1,0,5,4:T(8,128)}, u32[]{:S(2)}) copy-start(f32[2,2,2,8,2,12,64]{6,3,2,1,0,5,4:T(8,128)} %copy-done.18) | copy-start | bytes 1179652
  292.2 57.8 %collective-permute-start.5 = (f32[638976]{0:T(1024)S(1)}, f32[638976]{0:T(1024)S(1)}, u32[]{:S(2)}, u32[]{:S(2)}) collective-permute-start(f32[638976]{0:T(1024)S(1)} %pad_maximum_fusion.5), channel_id=1, source_target_pairs={{0,2},{1,3},{2,0},{3,1},{4,6},{5,7},{6,4},{7,5},{8,10},{9,11},{10,... | collective-permute-start | bytes 7667720 | tf_op jit(solution)/shard_map/ppermute | solution.py:22
  350.0 1.6 copy-start.7
  352.0 0.8 copy-start.24
  352.7 5.7 %copy-start.3 = (f32[2,2,2,32,2,12,64]{6,3,2,1,0,5,4:T(8,128)S(1)}, f32[2,2,2,32,2,12,64]{6,3,2,1,0,5,4:T(8,128)}, u32[]{:S(2)}) copy-start(f32[2,2,2,32,2,12,64]{6,3,2,1,0,5,4:T(8,128)} %copy-done.2) | copy-start | bytes 4718596
  361.0 1.2 copy-start.12
  362.3 1.4 slice-start.1
  366.2 4.4 %copy-start.5 = (f32[2,2,128,2,12,64]{2,5,4,3,1,0:T(8,128)S(1)}, f32[2,2,128,2,12,64]{2,5,4,3,1,0:T(8,128)}, u32[]{:S(2)}) copy-start(f32[2,2,128,2,12,64]{2,5,4,3,1,0:T(8,128)} %copy-done.4) | copy-start | bytes 9437188
  372.2 1.2 copy-start.8
  373.5 2.2 copy-start.27
  375.3 3.8 copy-start.31
  375.3 4.0 copy-start.35
  375.7 33.2 %copy-start.13 = (f32[2,2,32,2,12,64]{5,2,1,0,4,3:T(8,128)S(1)}, f32[2,2,32,2,12,64]{5,2,1,0,4,3:T(8,128)}, u32[]{:S(2)}) copy-start(f32[2,2,32,2,12,64]{5,2,1,0,4,3:T(8,128)} %copy-done.12) | copy-start | bytes 2359300
  376.8 30.3 %collective-permute-start.6 = (f32[319488]{0:T(1024)}, f32[319488]{0:T(1024)S(1)}, u32[]{:S(2)}, u32[]{:S(2)}) collective-permute-start(f32[319488]{0:T(1024)} %pad_maximum_fusion.9), channel_id=1, source_target_pairs={{0,4},{1,5},{2,6},{3,7},{4,0},{5,1},{6,2},{7,3},{8,12},{9,13},{10,... | collective-permute-start | bytes 3833864 | tf_op jit(solution)/shard_map/ppermute | solution.py:22
  407.1 1.5 copy-start.17
  409.3 0.9 copy-start.20
  411.3 8.0 %copy-start.25 = (bf16[128,12,64]{0,2,1:T(8,128)(2,1)S(1)}, bf16[128,12,64]{0,2,1:T(8,128)(2,1)}, u32[]{:S(2)}) copy-start(bf16[128,12,64]{0,2,1:T(8,128)(2,1)} %get-tuple-element.33) | copy-start | bytes 589828
  411.3 9.7 %slice-start.2 = ((f32[319488]{0:T(1024)}), f32[196608]{0:T(1024)S(1)}, s32[]{:S(2)}) async-start(f32[319488]{0:T(1024)} %copy-done.17), calls=%async_computation.2 | async-start | bytes 1572864 | tf_op jit(solution)/shard_map/slice | solution.py:131
  411.3 14.0 %collective-permute-start.7 = (f32[61440]{0:T(1024)}, f32[61440]{0:T(1024)}, u32[]{:S(2)}, u32[]{:S(2)}) collective-permute-start(f32[61440]{0:T(1024)} %pad_maximum_fusion.17), channel_id=1, source_target_pairs={{0,8},{1,9},{2,10},{3,11},{4,12},{5,13},{6,14},{7,15},{8,0},{9,1},... | collective-permute-start | bytes 737288 | tf_op jit(solution)/shard_map/ppermute | solution.py:22
  428.7 3.1 copy-start.9
  428.7 3.1 copy-start.33

commit v2 on v1

v2 whole, which is shorter than its diff:
```python
import math

import jax
import jax.numpy as jnp
from jax import lax
from jax.experimental import pallas as pl
from jax.experimental.pallas import tpu as pltpu
from jax.sharding import PartitionSpec as P

LEN_NEAR = 1024
LEN_MID = 4096
LEN_FAR = 16384
DILATION_FIRST = 1
DILATION_SECOND = 4
DILATION_THIRD = 16

NEG_FILL = -1e30
STRIDES = (DILATION_FIRST, DILATION_SECOND, DILATION_THIRD)


def exchange(block, bit):
    count = lax.axis_size("seq")
    route = [(index, index ^ (1 << bit)) for index in range(count)]
    return lax.ppermute(block, "seq", route)


def pick_rows(rows, stride, offsets_row):
    if stride == 1:
        return rows
    pair, count, width = rows.shape
    heads = offsets_row.shape[0]
    grouped = rows.reshape(pair, count // stride, stride, heads, width // heads)
    chosen = (jnp.arange(stride, dtype=jnp.int32)[:, None] == offsets_row[None, :])[
        None, None, :, :, None
    ]
    picked = jnp.sum(jnp.where(chosen, grouped, jnp.zeros((), rows.dtype)), axis=2)
    return picked.reshape(pair, count // stride, width)


def spread_rows(picked, stride, offsets_row):
    if stride == 1:
        return picked
    pair, count, width = picked.shape
    heads = offsets_row.shape[0]
    grouped = picked.reshape(pair, count, 1, heads, width // heads)
    chosen = (jnp.arange(stride, dtype=jnp.int32)[:, None] == offsets_row[None, :])[
        None, None, :, :, None
    ]
    widened = jnp.where(chosen, grouped, jnp.zeros((), picked.dtype))
    return widened.reshape(pair, count * stride, width)


def attention_kernel(key_counts, head_dim, score_scale):
    first_end = key_counts[0]
    second_end = key_counts[0] + key_counts[1]

    def kernel(offsets_ref, query_ref, key_ref, value_ref, grad_ref, out_ref, qgrad_ref, terms_ref):
        pair = pl.program_id(0)
        rows = query_ref.shape[0]
        keys = key_ref.shape[0]
        row_index = lax.broadcasted_iota(jnp.int32, (rows, keys), 0)
        col_index = lax.broadcasted_iota(jnp.int32, (rows, keys), 1)
        heads_per_block = query_ref.shape[1] // head_dim
        for sub in range(heads_per_block):
            head = pair * heads_per_block + sub
            cols = slice(sub * head_dim, (sub + 1) * head_dim)
            query = query_ref[:, cols]
            key = key_ref[:, cols]
            value = value_ref[:, cols]
            grad = grad_ref[:, cols]
            member = [
                (row_index % STRIDES[branch]) == offsets_ref[branch, head] for branch in range(3)
            ]
            in_first = col_index < first_end
            in_third = col_index >= second_end
            in_second = jnp.logical_not(in_first | in_third)
            valid = (in_first & member[0]) | (in_second & member[1]) | (in_third & member[2])
            scores = (
                lax.dot_general(
                    query, key, (((1,), (1,)), ((), ())), preferred_element_type=jnp.float32
                )
                * score_scale
            )
            scores = jnp.where(valid, scores, NEG_FILL)
            peak = jnp.max(scores, axis=1, keepdims=True)
            expo = jnp.where(valid, jnp.exp(scores - peak), 0.0)
            total = jnp.sum(expo, axis=1, keepdims=True)
            prob = expo / total
            weight = prob.astype(jnp.bfloat16)
            mixed = jnp.dot(weight, value, preferred_element_type=jnp.float32)
            out_ref[:, cols] = mixed.astype(out_ref.dtype)
            balance = jnp.sum(grad.astype(jnp.float32) * mixed, axis=1, keepdims=True)
            flow = lax.dot_general(
                grad, value, (((1,), (1,)), ((), ())), preferred_element_type=jnp.float32
            )
            score_grad_wide = prob * (flow - balance)
            score_grad = score_grad_wide.astype(jnp.bfloat16)
            query_grad = jnp.dot(score_grad, key, preferred_element_type=jnp.float32) * score_scale
            qgrad_ref[:, cols] = query_grad.astype(qgrad_ref.dtype)
            key_terms = (
                jnp.dot(
                    jnp.transpose(score_grad_wide).astype(jnp.bfloat16),
                    query,
                    preferred_element_type=jnp.float32,
                )
                * score_scale
            )
            value_terms = jnp.dot(
                jnp.transpose(prob).astype(jnp.bfloat16), grad, preferred_element_type=jnp.float32
            )
            terms_ref[0, :, cols] = key_terms
            terms_ref[1, :, cols] = value_terms

    return kernel


def make_per_device(branch_bits):
    top_bits = max(branch_bits)

    def per_device(query_rows, key_rows, value_rows, output_grad, head_offsets):
        local_rows, model_width = query_rows.shape
        head_count = head_offsets.shape[1]
        head_dim = model_width // head_count
        score_scale = 1.0 / math.sqrt(head_dim)
        kv_rows = jnp.stack([key_rows, value_rows])

        buffers = [
            pick_rows(kv_rows, STRIDES[branch], head_offsets[branch]) for branch in range(3)
        ]
        for bit in reversed(range(top_bits)):
            active = [branch for branch in range(3) if branch_bits[branch] > bit]
            outgoing = jnp.concatenate([buffers[branch].reshape(-1) for branch in active])
            incoming = exchange(outgoing, bit)
            cursor = 0
            for branch in active:
                size = buffers[branch].size
                arrived = incoming[cursor : cursor + size].reshape(buffers[branch].shape)
                cursor += size
                buffers[branch] = jnp.stack([buffers[branch], arrived], axis=1)
        gathered = [
            buffers[branch].reshape(2, -1, model_width) for branch in range(3)
        ]
        key_counts = [block.shape[1] for block in gathered]
        kv_all = jnp.concatenate(gathered, axis=1)
        key_total = kv_all.shape[1]

        block_width = 128 if (128 % head_dim == 0 and model_width % 128 == 0) else model_width
        pairs = model_width // block_width
        row_block = pl.BlockSpec((local_rows, block_width), lambda p, offs: (0, p))
        key_block = pl.BlockSpec((key_total, block_width), lambda p, offs: (0, p))
        attended, query_grad, terms = pl.pallas_call(
            attention_kernel(key_counts, head_dim, score_scale),
            out_shape=(
                jax.ShapeDtypeStruct((local_rows, model_width), jnp.bfloat16),
                jax.ShapeDtypeStruct((local_rows, model_width), jnp.bfloat16),
                jax.ShapeDtypeStruct((2, key_total, model_width), jnp.float32),
            ),
            grid_spec=pltpu.PrefetchScalarGridSpec(
                num_scalar_prefetch=1,
                grid=(pairs,),
                in_specs=[row_block, key_block, key_block, row_block],
                out_specs=[
                    row_block,
                    row_block,
                    pl.BlockSpec((2, key_total, block_width), lambda p, offs: (0, 0, p)),
                ],
            ),
            compiler_params=pltpu.CompilerParams(vmem_limit_bytes=100 * 1024 * 1024),
        )(head_offsets, query_rows, kv_all[0], kv_all[1], output_grad)

        starts = [0, key_counts[0], key_counts[0] + key_counts[1], key_total]
        partial = []
        for branch in range(3):
            block = terms[:, starts[branch] : starts[branch + 1]]
            partial.append(block.reshape((2,) + (2,) * branch_bits[branch] + (-1, model_width)))
        for bit in range(top_bits):
            active = [branch for branch in range(3) if branch_bits[branch] > bit]
            outgoing = jnp.concatenate([partial[branch][:, 1].reshape(-1) for branch in active])
            incoming = exchange(outgoing, bit)
            cursor = 0
            for branch in active:
                kept = partial[branch][:, 0]
                size = kept.size
                partial[branch] = kept + incoming[cursor : cursor + size].reshape(kept.shape)
                cursor += size
        total_grad = None
        for branch in range(3):
            spread = spread_rows(partial[branch], STRIDES[branch], head_offsets[branch])
            total_grad = spread if total_grad is None else total_grad + spread

        return (
            attended,
            query_grad,
            total_grad[0].astype(jnp.bfloat16),
            total_grad[1].astype(jnp.bfloat16),
        )

    return per_device


def solution(mesh):
    group_count = mesh.shape["groups"]
    seq_devices = mesh.shape["seq"]

    def run(query_rows, key_rows, value_rows, output_grad, head_offsets):
        local_rows = query_rows.shape[0] // (group_count * seq_devices)
        tokens_all = seq_devices * local_rows
        seg_lengths = [min(LEN_NEAR, tokens_all), min(LEN_MID, tokens_all), min(LEN_FAR, tokens_all)]
        branch_bits = [(seg_length // local_rows).bit_length() - 1 for seg_length in seg_lengths]
        row_spec = P(("groups", "seq"), None)
        return jax.shard_map(
            make_per_device(branch_bits),
            mesh=mesh,
            in_specs=(row_spec, row_spec, row_spec, row_spec, P()),
            out_specs=(row_spec, row_spec, row_spec, row_spec),
            check_vma=False,
        )(query_rows, key_rows, value_rows, output_grad, head_offsets)

    return run
```

time: 444 us -> 318 us (0.72); the launches traced: 436 us -> 317 us
  local copies, waits for them, and re-layouts: 184 us -> 89.4 us
  other arithmetic: 70.6 us -> 36 us
  matrix products: 30.8 us -> 0 us
  Pallas kernels: 0 us -> 23.5 us
  waiting for transfers between devices: 134 us -> 152 us
    another operation x48 -> x38, local copies, waits for them, and re-layouts: 59.7 us -> 22.5 us  [the longest x11 10.7 us: per_device(): partial[branch][:, 1].reshape(-1)]
    pallas_call x0 -> x1, Pallas kernels: none -> 23.5 us  [per_device(): pl.pallas_call(attention_kernel(key_counts, head_dim, score_scale), out_s...]
    reshape x14 -> x7, local copies, waits for them, and re-layouts: 31 us -> 11.2 us  [per_device(): partial[branch] = kept + incoming[cursor:cursor + size].reshape(kept.shape)]
    ppermute x8, waiting for transfers between devices: 134 us -> 152 us  [exchange(): return lax.ppermute(block, 'seq', route)]
    slice x22 -> x16, local copies, waits for them, and re-layouts: 32.7 us -> 16.8 us  [the longest x3 9.4 us: per_device(): block = terms[:, starts[branch]:starts[branch + 1]]]
    dot_general x5 -> x0, matrix products: 15.6 us -> none  [the longest x1 5.28 us: per_device(): jnp.einsum('qhe,khe->hqk', grad3, value_all, preferred_element_type=jnp.f...]
    sub x1 -> x0, matrix products: 15.2 us -> none  [per_device(): expo = jnp.where(valid, jnp.exp(scores - peak), 0.0)]
    another operation x14 -> x10, other arithmetic: 15.7 us -> 5.86 us  [per_device(): buffers[branch] = jnp.stack([buffers[branch], arrived], axis=1)]
  transfers between devices with their start and end apart: 8 -> 8, of which waited for: 7 -> 8; matrix products, arithmetic and copies ran while one was open for 5% -> 1% of each run, Pallas kernels for 0% -> 0%
where the time goes in v2:
time: 318 us; the launch traced here: 317 us
  waiting for transfers between devices  152 us (48%)
  local copies, waits for them, and re-layouts  89.4 us (28%)
  other arithmetic  36 us (11%)
  Pallas kernels  23.5 us (7%)
  starting transfers between devices  13.9 us (4%)
    ppermute x8, waiting for transfers between devices, exchange(): return lax.ppermute(block, 'seq', route)  152 us
    pallas_call x1, Pallas kernels, per_device(): pl.pallas_call(attention_kernel(key_counts, head_dim, score_scale), out_s...  23.5 us
    ppermute x8, starting transfers between devices, exchange(): return lax.ppermute(block, 'seq', route)  13.9 us
    add x10, other arithmetic, per_device(): partial[branch] = kept + incoming[cursor:cursor + size].reshape(kept.shape)  11.9 us
    slice x15, local copies, waits for them, and re-layouts, per_device(): partial[branch] = kept + incoming[cursor:cursor + size].reshape(kept.shape)  11.6 us
    reshape x7, local copies, waits for them, and re-layouts, per_device(): partial[branch] = kept + incoming[cursor:cursor + size].reshape(kept.shape)  11.2 us
    another operation x11, local copies, waits for them, and re-layouts, per_device(): partial[branch][:, 1].reshape(-1)  10.7 us
    unnamed x40, local copies, waits for them, and re-layouts  9.59 us
  transfers between devices with their start and end apart: 8, of which 8 were waited for; matrix products, arithmetic and copies ran while one was open for 1% of the time, Pallas kernels for 0%

profile of v2, /device:TPU:0, one launch (start us, length us, event | category | flops | bytes accessed | tf_op | source)
XLA Modules:
  0.0 316.9 jit_solution(12513816030254439943)
XLA Ops:
  0.6 1.3 stack.88
  1.9 1.3 stack.85
  3.3 1.3 stack.89
  4.5 1.3 stack.86
  7.6 4.1 %collective-permute-start = (bf16[61440]{0:T(1024)(128)(2,1)S(1)}, bf16[61440]{0:T(1024)(128)(2,1)S(1)}, u32[]{:S(2)}, u32[]{:S(2)}) collective-permute-start(bf16[61440]{0:T(1024)(128)(2,1)S(1)} %pad_maximum_fusion.17), channel_id=1, source_target_pairs={{0,8},{1,9},{2,10},{3,11},{4,12},{5,13},{6,14},{7,15},{8,0},{9,1},... | collective-permute-start | bytes 368648 | tf_op jit(solution)/shard_map/ppermute | solution.py:24
  12.5 5.2 %collective-permute-done = bf16[61440]{0:T(1024)(128)(2,1)S(1)} collective-permute-done((bf16[61440]{0:T(1024)(128)(2,1)S(1)}, bf16[61440]{0:T(1024)(128)(2,1)S(1)}, u32[]{:S(2)}, u32[]{:S(2)}) %collective-permute-start) | collective-permute-done | bytes 122912 | tf_op jit(solution)/shard_map/ppermute | solution.py:24
  19.0 14.9 %collective-permute-done.1 = bf16[319488]{0:T(1024)(128)(2,1)S(1)} collective-permute-done((bf16[319488]{0:T(1024)(128)(2,1)S(1)}, bf16[319488]{0:T(1024)(128)(2,1)S(1)}, u32[]{:S(2)}, u32[]{:S(2)}) %collective-permute-start.1) | collective-permute-done | bytes 639008 | tf_op jit(solution)/shard_map/ppermute | solution.py:24
  36.1 1.3 collective-permute-start.2
  37.4 27.1 %collective-permute-done.2 = bf16[638976]{0:T(1024)(128)(2,1)S(1)} collective-permute-done((bf16[638976]{0:T(1024)(128)(2,1)S(1)}, bf16[638976]{0:T(1024)(128)(2,1)S(1)}, u32[]{:S(2)}, u32[]{:S(2)}) %collective-permute-start.2) | collective-permute-done | bytes 1277984 | tf_op jit(solution)/shard_map/ppermute | solution.py:24
  64.5 1.1 copy-done.11
  65.9 1.2 slice.309
  68.2 1.1 fusion.19
  69.3 1.6 reshape.225
  70.9 1.4 fusion.21
  72.4 1.3 reshape.224
  73.7 9.0 %pad_maximum_fusion.3 = bf16[1277952]{0:T(1024)(128)(2,1)S(1)} fusion(bf16[98304]{0:T(1024)(128)(2,1)S(1)} %reshape.226, bf16[393216]{0:T(1024)(128)(2,1)} %reshape.225, bf16[786432]{0:T(1024)(128)(2,1)S(1)} %reshape.224), kind=kLoop, calls=%fused_computation.7 | loop fusion | flops 7667712 | bytes 5111808 | tf_op jit(solution)/shard_map/concatenate | solution.py:132
  82.8 4.8 %collective-permute-done.3 = bf16[1277952]{0:T(1024)(128)(2,1)S(1)} collective-permute-done((bf16[1277952]{0:T(1024)(128)(2,1)S(1)}, bf16[1277952]{0:T(1024)(128)(2,1)S(1)}, u32[]{:S(2)}, u32[]{:S(2)}) %collective-permute-start.3) | collective-permute-done | bytes 2555936 | tf_op jit(solution)/shard_map/ppermute | solution.py:24
  87.6 1.4 copy-done.7
  89.3 1.5 slice.312
  90.8 1.4 stack_reshape.38
  92.2 1.6 pad_maximum_fusion.2
  94.1 2.1 slice.313
  96.1 2.5 stack_reshape.39
  98.6 1.5 pad_maximum_fusion.6
  100.6 2.6 slice_bitcast_fusion.1
  103.3 23.5 %shard_map.84 = (bf16[128,768]{1,0:T(8,128)(2,1)}, bf16[128,768]{1,0:T(8,128)(2,1)}, f32[2,1664,768]{2,1,0:T(8,128)}) custom-call(s32[3,12]{1,0:T(4,128)} %offsets_ref.1, bf16[128,768]{1,0:T(8,128)(2,1)} %query_ref.1, bf16[1664,768]{1,0:T(8,128)(2,1)} %get-tuple-element.11.key_ref, bf16[1664,768]{1,0:T(8,128)(2,1)} %get-tuple-element.10.value_ref, ...), custom_call_target="tpu_custom_call" | custom-call | tf_op jit(solution)/shard_map/pallas_call | solution.py:151
  126.8 1.2 slice.267
  128.0 2.4 slice.265
  130.3 5.8 %slice.262 = f32[2,1024,768]{2,1,0:T(8,128)} slice(f32[2,1664,768]{2,1,0:T(8,128)} %get-tuple-element.9), slice={[0:2], [0:1024], [0:768]} | slice | bytes 12582912 | tf_op jit(solution)/shard_map/slice | solution.py:174
  136.9 1.0 reshape_squeeze.35
  138.0 1.3 slice.319
  139.3 2.5 reshape_squeeze.34
  141.8 3.8 %slice.318 = f32[2,1,2,2,128,768]{5,4,3,2,1,0:T(8,128)} slice(f32[2,2,2,2,128,768]{5,4,3,2,1,0:T(8,128)} %bitcast.128), slice={[0:2], [1:2], [0:2], [0:2], [0:128], [0:768]} | slice | bytes 6291456 | tf_op jit(solution)/shard_map/slice | solution.py:178
  145.6 4.4 %reshape_squeeze.33 = f32[786432]{0:T(1024)} reshape(f32[2,1,2,2,128,768]{5,4,3,2,1,0:T(8,128)} %slice.318) | data formatting | bytes 6291456 | tf_op jit(solution)/shard_map/reshape;squeeze | solution.py:178
  150.0 4.5 %pad_maximum_fusion.1 = f32[1277952]{0:T(1024)S(1)} fusion(f32[98304]{0:T(1024)S(1)} %reshape_squeeze.35, f32[393216]{0:T(1024)} %reshape_squeeze.34, f32[786432]{0:T(1024)} %reshape_squeeze.33), kind=kLoop, calls=%fused_computation.1 | loop fusion | flops 2555904 | bytes 10223616 | tf_op jit(solution)/shard_map/concatenate | solution.py:178
  154.7 8.3 %collective-permute-done.4 = f32[1277952]{0:T(1024)S(1)} collective-permute-done((f32[1277952]{0:T(1024)S(1)}, f32[1277952]{0:T(1024)S(1)}, u32[]{:S(2)}, u32[]{:S(2)}) %collective-permute-start.4) | collective-permute-done | bytes 5111840 | tf_op jit(solution)/shard_map/ppermute | solution.py:24
  163.0 2.3 copy-done.3
  166.2 1.2 fusion.11
  168.0 1.6 reshape_squeeze.38
  169.6 3.7 %slice.321 = f32[786432]{0:T(1024)} slice(f32[1277952]{0:T(1024)} %copy-done.3), slice={[0:786432]} | slice | bytes 6291456 | tf_op jit(solution)/shard_map/slice | solution.py:184
  173.4 4.6 %reshape.233 = f32[2,2,2,128,768]{4,3,2,1,0:T(8,128)} reshape(f32[786432]{0:T(1024)} %slice.321) | data formatting | bytes 6291456 | tf_op jit(solution)/shard_map/reshape | solution.py:184
  178.0 4.9 %fusion = f32[2,2,2,128,768]{4,3,2,1,0:T(8,128)} fusion(f32[2,2,2,128,768]{4,3,2,1,0:T(8,128)} %reshape.233, f32[2,2,2,2,128,768]{5,4,3,2,1,0:T(8,128)} %bitcast.129), kind=kLoop, calls=%fused_computation.3 | loop fusion | flops 786432 | bytes 9437184 | tf_op jit(solution)/shard_map/add | solution.py:184
  182.9 2.7 slice.325
  185.6 2.6 reshape.234
  188.2 1.6 fusion.1
  189.8 1.1 copy-done.1
  191.0 0.9 reshape_squeeze.37
  192.8 1.4 pad_maximum_fusion.4
  194.2 1.3 collective-permute-start.5
  195.6 56.2 %collective-permute-done.5 = f32[638976]{0:T(1024)S(1)} collective-permute-done((f32[638976]{0:T(1024)S(1)}, f32[638976]{0:T(1024)S(1)}, u32[]{:S(2)}, u32[]{:S(2)}) %collective-permute-start.5) | collective-permute-done | bytes 2555936 | tf_op jit(solution)/shard_map/ppermute | solution.py:24
  251.8 1.5 copy-done.8
  254.1 2.8 slice.330
  256.9 2.6 reshape.235
  259.5 2.8 fusion.2
  262.3 1.3 slice.334
  263.6 1.0 reshape.236
  264.6 1.3 fusion.5
  267.0 2.3 collective-permute-start.6
  269.4 27.5 %collective-permute-done.6 = f32[319488]{0:T(1024)S(1)} collective-permute-done((f32[319488]{0:T(1024)S(1)}, f32[319488]{0:T(1024)S(1)}, u32[]{:S(2)}, u32[]{:S(2)}) %collective-permute-start.6) | collective-permute-done | bytes 1277984 | tf_op jit(solution)/shard_map/ppermute | solution.py:24
  297.3 3.8 %collective-permute-start.7 = (f32[61440]{0:T(1024)S(1)}, f32[61440]{0:T(1024)S(1)}, u32[]{:S(2)}, u32[]{:S(2)}) collective-permute-start(f32[61440]{0:T(1024)S(1)} %pad_maximum_fusion.15), channel_id=1, source_target_pairs={{0,8},{1,9},{2,10},{3,11},{4,12},{5,13},{6,14},{7,15},{8,0},{9,1},... | collective-permute-start | bytes 737288 | tf_op jit(solution)/shard_map/ppermute | solution.py:24
  302.5 8.4 %collective-permute-done.7 = f32[61440]{0:T(1024)S(1)} collective-permute-done((f32[61440]{0:T(1024)S(1)}, f32[61440]{0:T(1024)S(1)}, u32[]{:S(2)}, u32[]{:S(2)}) %collective-permute-start.7) | collective-permute-done | bytes 245792 | tf_op jit(solution)/shard_map/ppermute | solution.py:24
  311.4 1.4 broadcast_in_dim.92
  312.9 1.4 broadcast_in_dim.99
  314.3 1.8 fusion.9
  (141 shorter events, 16.6 us)
Async XLA Ops:
  0.6 5.2 %copy-start.16 = (s32[3,12]{1,0:T(4,128)S(1)}, s32[3,12]{1,0:T(4,128)}, u32[]{:S(2)}) copy-start(s32[3,12]{1,0:T(4,128)} %offsets_ref.1) | copy-start | bytes 436
  1.9 9.9 %copy-start.9 = (bf16[128,768]{1,0:T(8,128)(2,1)S(1)}, bf16[128,768]{1,0:T(8,128)(2,1)}, u32[]{:S(2)}) copy-start(bf16[128,768]{1,0:T(8,128)(2,1)} %param.7) | copy-start | bytes 589828
  1.9 9.9 %copy-start.10 = (bf16[128,768]{1,0:T(8,128)(2,1)S(1)}, bf16[128,768]{1,0:T(8,128)(2,1)}, u32[]{:S(2)}) copy-start(bf16[128,768]{1,0:T(8,128)(2,1)} %param.6) | copy-start | bytes 589828
  5.8 1.6 copy-start.17
  5.9 0.6 copy-start.14
  7.6 10.1 %collective-permute-start = (bf16[61440]{0:T(1024)(128)(2,1)S(1)}, bf16[61440]{0:T(1024)(128)(2,1)S(1)}, u32[]{:S(2)}, u32[]{:S(2)}) collective-permute-start(bf16[61440]{0:T(1024)(128)(2,1)S(1)} %pad_maximum_fusion.17), channel_id=1, source_target_pairs={{0,8},{1,9},{2,10},{3,11},{4,12},{5,13},{6,14},{7,15},{8,0},{9,1},... | collective-permute-start | bytes 368648 | tf_op jit(solution)/shard_map/ppermute | solution.py:24
  18.2 15.6 %collective-permute-start.1 = (bf16[319488]{0:T(1024)(128)(2,1)S(1)}, bf16[319488]{0:T(1024)(128)(2,1)S(1)}, u32[]{:S(2)}, u32[]{:S(2)}) collective-permute-start(bf16[319488]{0:T(1024)(128)(2,1)S(1)} %pad_maximum_fusion.11), channel_id=1, source_target_pairs={{0,4},{1,5},{2,6},{3,7},{4,0},{5,1},{6,2},{7,3},{8,12},{9,13},{10,... | collective-permute-start | bytes 1916936 | tf_op jit(solution)/shard_map/ppermute | solution.py:24
  36.1 28.4 %collective-permute-start.2 = (bf16[638976]{0:T(1024)(128)(2,1)S(1)}, bf16[638976]{0:T(1024)(128)(2,1)S(1)}, u32[]{:S(2)}, u32[]{:S(2)}) collective-permute-start(bf16[638976]{0:T(1024)(128)(2,1)S(1)} %pad_maximum_fusion.7), channel_id=1, source_target_pairs={{0,2},{1,3},{2,0},{3,1},{4,6},{5,7},{6,4},{7,5},{8,10},{9,11},{10,... | collective-permute-start | bytes 3833864 | tf_op jit(solution)/shard_map/ppermute | solution.py:24
  64.5 1.1 copy-start.11
  65.7 2.1 slice-start.2
  82.7 4.9 %collective-permute-start.3 = (bf16[1277952]{0:T(1024)(128)(2,1)S(1)}, bf16[1277952]{0:T(1024)(128)(2,1)S(1)}, u32[]{:S(2)}, u32[]{:S(2)}) collective-permute-start(bf16[1277952]{0:T(1024)(128)(2,1)S(1)} %pad_maximum_fusion.3), channel_id=1, source_target_pairs={{0,1},{1,0},{2,3},{3,2},{4,5},{5,4},{6,7},{7,6},{8,9},{9,8},{10,11... | collective-permute-start | bytes 7667720 | tf_op jit(solution)/shard_map/ppermute | solution.py:24
  87.6 1.4 copy-start.7
  127.9 8.2 %copy-start.4 = (f32[2,128,768]{2,1,0:T(8,128)}, f32[2,128,768]{2,1,0:T(8,128)S(1)}, u32[]{:S(2)}) copy-start(f32[2,128,768]{2,1,0:T(8,128)S(1)} %slice.267) | copy-start | bytes 2359300
  154.5 8.5 %collective-permute-start.4 = (f32[1277952]{0:T(1024)S(1)}, f32[1277952]{0:T(1024)S(1)}, u32[]{:S(2)}, u32[]{:S(2)}) collective-permute-start(f32[1277952]{0:T(1024)S(1)} %pad_maximum_fusion.1), channel_id=1, source_target_pairs={{0,1},{1,0},{2,3},{3,2},{4,5},{5,4},{6,7},{7,6},{8,9},{9,8},{10,11... | collective-permute-start | bytes 15335432 | tf_op jit(solution)/shard_map/ppermute | solution.py:24
  163.0 2.3 copy-start.3
  189.8 1.2 copy-start.1
  191.0 1.7 slice-start
  194.2 57.6 %collective-permute-start.5 = (f32[638976]{0:T(1024)S(1)}, f32[638976]{0:T(1024)S(1)}, u32[]{:S(2)}, u32[]{:S(2)}) collective-permute-start(f32[638976]{0:T(1024)S(1)} %pad_maximum_fusion.4), channel_id=1, source_target_pairs={{0,2},{1,3},{2,0},{3,1},{4,6},{5,7},{6,4},{7,5},{8,10},{9,11},{10,... | collective-permute-start | bytes 7667720 | tf_op jit(solution)/shard_map/ppermute | solution.py:24
  251.8 1.5 copy-start.8
  253.4 0.7 copy-start.12
  254.1 5.4 %copy-start = (f32[2,2,2,128,768]{4,3,2,1,0:T(8,128)S(1)}, f32[2,2,2,128,768]{4,3,2,1,0:T(8,128)}, u32[]{:S(2)}) copy-start(f32[2,2,2,128,768]{4,3,2,1,0:T(8,128)} %fusion) | copy-start | bytes 9437188
  262.3 2.3 copy-start.2
  264.6 2.2 slice-start.1
  265.9 0.9 copy-start.5
  266.9 30.1 %copy-start.13 = (f32[2,2,2,8,768]{4,3,2,1,0:T(8,128)S(1)}, f32[2,2,2,8,768]{4,3,2,1,0:T(8,128)}, u32[]{:S(2)}) copy-start(f32[2,2,2,8,768]{4,3,2,1,0:T(8,128)} %copy-done.12) | copy-start | bytes 589828
  266.9 30.2 %copy-start.6 = (f32[2,2,2,32,768]{4,3,2,1,0:T(8,128)S(1)}, f32[2,2,2,32,768]{4,3,2,1,0:T(8,128)}, u32[]{:S(2)}) copy-start(f32[2,2,2,32,768]{4,3,2,1,0:T(8,128)} %copy-done.5) | copy-start | bytes 2359300
  267.0 29.9 %collective-permute-start.6 = (f32[319488]{0:T(1024)S(1)}, f32[319488]{0:T(1024)S(1)}, u32[]{:S(2)}, u32[]{:S(2)}) collective-permute-start(f32[319488]{0:T(1024)S(1)} %pad_maximum_fusion.8), channel_id=1, source_target_pairs={{0,4},{1,5},{2,6},{3,7},{4,0},{5,1},{6,2},{7,3},{8,12},{9,13},{10,... | collective-permute-start | bytes 3833864 | tf_op jit(solution)/shard_map/ppermute | solution.py:24
  296.9 4.2 %copy-start.15 = (pred[16,12]{1,0:T(8,128)(4,1)S(1)}, pred[16,12]{1,0:T(8,128)(4,1)}, u32[]{:S(2)}) copy-start(pred[16,12]{1,0:T(8,128)(4,1)} %copy-done.14) | copy-start | bytes 580
  297.0 4.6 %copy-start.18 = (pred[4,12]{1,0:T(4,128)(4,1)S(1)}, pred[4,12]{1,0:T(4,128)(4,1)}, u32[]{:S(2)}) copy-start(pred[4,12]{1,0:T(4,128)(4,1)} %copy-done.17) | copy-start | bytes 148
  297.3 13.6 %collective-permute-start.7 = (f32[61440]{0:T(1024)S(1)}, f32[61440]{0:T(1024)S(1)}, u32[]{:S(2)}, u32[]{:S(2)}) collective-permute-start(f32[61440]{0:T(1024)S(1)} %pad_maximum_fusion.15), channel_id=1, source_target_pairs={{0,8},{1,9},{2,10},{3,11},{4,12},{5,13},{6,14},{7,15},{8,0},{9,1},... | collective-permute-start | bytes 737288 | tf_op jit(solution)/shard_map/ppermute | solution.py:24
